TPU v7x, 128 devices: a whole 4x4x4 slice. The times are simulated.
128 devices in a mesh: grp: 8 (over y, core), shard: 16 (over z, x).
Axes of the slice: x: 4, y: 4, z: 4, core: 2. Of those that a mesh axis runs over, the one named last changes fastest.
Arguments:
- tokens: bfloat16 [65536, 2560], P(('grp', 'shard')), may hold values from -6 to 6
- gain: float32 [2560], replicated, may hold values from 0.25 to 1.75
- w_qkv: bfloat16 [2560, 3072], P(None, 'shard'), may hold values from -1 to 1
- prefix_kv: bfloat16 [8, 2048, 512], P('grp', 'shard'), may hold values from -6 to 6
- prefix_owner: int32 [8], P('grp'), may hold values from 0 to 7, as said below
- suffix_len: int32 [8, 16], P('grp', 'shard'), may hold values from 1 to 512, 5120 in all within a row
- slots: int32 [8, 8192], P('grp', 'shard'), may hold values from 0 to 8191, as said below
Outputs:
- attended: bfloat16 [65536, 2560], P(('grp', 'shard'))
Inputs may be any that keep to these rules, and one draw needn't show every extreme that they name: In each group the slots are a permutation of 0 to 8191; in each aligned run of 512 entries the k-th block of 32 entries holds slots k * 512 to (k + 1) * 512 - 1. `suffix_len`: each group's lengths sum to 5120 and one of them equals 512. `prefix_owner`: each entry names one of the 8 caches; several groups may name the same one.
All inputs are finite; a program needn't handle non-finite values.
Results may differ from a plain program's by a relative error of at most 0.0069.
Values may be sent and summed in bfloat16 or wider, within the bound.
No kernel may reach another device: no remote copies, remote signals or barrier semaphores. Data moves between devices by JAX's collectives and lax.ppermute only.
A program may use at most 128 MiB of HBM per device.

v0:
```python
import jax
import jax.numpy as jnp
from jax import lax
from jax.sharding import PartitionSpec as P

H = 10
HD = 256
WINDOW = 2048
SUF = 512
HQ = 2560


def normalize(rows, gain):
    rows32 = rows.astype(jnp.float32)
    factor = lax.rsqrt(jnp.mean(rows32 * rows32, axis=-1, keepdims=True) + 1e-06)
    return (rows32 * factor * gain).astype(jnp.bfloat16)


def attend_request(queries, suffix_kv, prefix, length):
    keys = jnp.concatenate([prefix[:, :HD], suffix_kv[:, :HD]], axis=0)
    values = jnp.concatenate([prefix[:, HD:], suffix_kv[:, HD:]], axis=0)
    span = keys.shape[0]
    prefix_len = prefix.shape[0]
    count = queries.shape[0]
    query_pos = jnp.arange(count, dtype=jnp.int32)[:, None]
    key_pos = jnp.arange(span, dtype=jnp.int32)[None, :]
    visible = (
        (key_pos > prefix_len + query_pos - WINDOW)
        & (key_pos <= prefix_len + query_pos)
        & (key_pos < prefix_len + length)
    )
    heads = queries.reshape(count, H, HD).transpose(1, 0, 2)

    def one_head(head_q):
        scores = jnp.dot(head_q, keys.T, preferred_element_type=jnp.float32) * HD ** (-0.5)
        scores = jnp.where(visible, scores, -1e30)
        top = jnp.max(scores, axis=-1, keepdims=True)
        expd = jnp.exp(scores - top)
        weights = (expd / jnp.sum(expd, axis=-1, keepdims=True)).astype(jnp.bfloat16)
        return jnp.dot(weights, values, preferred_element_type=jnp.float32)

    result = lax.map(one_head, heads).transpose(1, 0, 2).reshape(count, H * HD)
    return jnp.where(query_pos < length, result, 0.0).astype(jnp.bfloat16)


def gather_by_a2a(piece, axis_name, count):
    spread = jnp.broadcast_to(piece[None], (count,) + piece.shape)
    return lax.all_to_all(spread, axis_name, 0, 0, tiled=True)


def shards(tokens, gain, w_qkv, prefix_kv, prefix_owner, suffix_len, slots):
    tok_dev = tokens.shape[0]
    n_grp = lax.axis_size("grp")
    n_shard = lax.axis_size("shard")
    grp = lax.axis_index("grp")
    core = grp % 2
    pairs = [(g, g ^ 1) for g in range(n_grp)]
    normed = normalize(tokens, gain)
    partner_rows = lax.ppermute(normed, "grp", pairs)
    cols = w_qkv.shape[1]
    half = cols // 2
    w_mine = lax.dynamic_slice_in_dim(w_qkv, core * half, half, axis=1)
    w_gathered = lax.all_gather(w_mine, "shard", axis=1, tiled=True)
    both = jnp.concatenate([normed, partner_rows], axis=0)
    out = jnp.dot(both, w_gathered, preferred_element_type=jnp.float32).astype(jnp.bfloat16)
    out_mine = out[:tok_dev]
    out_back = lax.ppermute(out[tok_dev:], "grp", pairs)
    is0 = core == 0
    half0 = jnp.where(is0, out_mine, out_back).reshape(tok_dev, n_shard, 1, half)
    half1 = jnp.where(is0, out_back, out_mine).reshape(tok_dev, n_shard, 1, half)
    projected = jnp.concatenate([half0, half1], axis=2).reshape(tok_dev, n_shard * cols)
    order = slots.reshape(tok_dev)
    arrived, order = (
        lax.all_to_all(projected, "shard", split_axis=0, concat_axis=0, tiled=True),
        lax.all_to_all(order, "shard", split_axis=0, concat_axis=0, tiled=True),
    )
    first_slot = lax.axis_index("shard") * tok_dev
    pos = order - first_slot
    onehot = (jnp.arange(tok_dev, dtype=jnp.int32)[:, None] == pos[None, :]).astype(jnp.bfloat16)
    placed = jnp.dot(onehot, arrived, preferred_element_type=jnp.float32).astype(jnp.bfloat16)
    owner = prefix_owner[0]
    sliced = gather_by_a2a(prefix_kv[0], "grp", n_grp)
    chosen = lax.dynamic_index_in_dim(sliced, owner, 0, keepdims=False)
    prefix = gather_by_a2a(chosen, "shard", n_shard).reshape(-1, chosen.shape[-1])
    lengths = suffix_len.reshape(-1)
    results = attend_request(placed[:, :HQ], placed[:, HQ:], prefix, lengths[0])
    return results


def solution(mesh):
    return jax.shard_map(
        shards,
        mesh=mesh,
        in_specs=(
            P(("grp", "shard"), None),
            P(),
            P(None, "shard"),
            P("grp", "shard", None),
            P("grp"),
            P("grp", "shard"),
            P("grp", "shard"),
        ),
        out_specs=P(("grp", "shard"), None),
        check_vma=False,
    )
```

profile of v0, /device:TPU:0, one launch (start us, length us, event | category | flops | bytes accessed | tf_op | source)
XLA Modules:
  0.0 301.8 jit_solution(2866371976029989938)
XLA Ops:
  14.3 4.7 %all-to-all-start.2 = ((bf16[8,128,512]{2,1,0:T(8,128)(2,1)}), bf16[8,128,512]{2,1,0:T(8,128)(2,1)S(1)}, u32[]{:S(2)}, u32[]{:S(2)}) async-start(bf16[8,128,512]{2,1,0:T(8,128)(2,1)} %broadcast_in_dim.49), calls=%async_computation.2 | async-start | bytes 2097152 | tf_op jit(solution)/shard_map/all_to_all | solution.py:48
  19.0 61.6 %all-gather.2.cloned.1.call-done = bf16[2560,1536]{0,1:T(8,128)(2,1)} async-done(((bf16[2560,96]{0,1:T(8,128)(2,1)}), bf16[2560,1536]{0,1:T(8,128)(2,1)}) %all-gather.2.cloned.1.call-update) | async-done | bytes 7864336 | tf_op jit(solution)/shard_map/all_gather | solution.py:63
  80.6 12.2 %fusion.19 = bf16[1024,1536]{1,0:T(8,128)(2,1)S(1)} fusion(bf16[2560,1536]{0,1:T(8,128)(2,1)} %all-gather.2.cloned.1.call-done, bf16[512,2560]{1,0:T(8,128)(2,1)} %collective-permute-done, bf16[512,2560]{1,0:T(8,128)(2,1)} %fusion.13), kind=kOutput, calls=%fused_computation.27 | convolution fusion | flops 8065122304 | bytes 16252928 | tf_op jit(solution)/shard_map/dot_general | solution.py:65
  98.3 5.3 %all-to-all-start = ((s32[16,32,1]{1,2,0:T(1,128)}), s32[16,32,1]{1,2,0:T(1,128)S(1)}, u32[]{:S(2)}, u32[]{:S(2)}) async-start(s32[16,32,1]{1,2,0:T(1,128)} %all_to_all.20), calls=%async_computation | async-start | bytes 16384 | tf_op jit(solution)/shard_map/all_to_all | solution.py:75
  103.6 7.5 %all-to-all-done = s32[16,32,1]{1,2,0:T(1,128)S(1)} async-done(((s32[16,32,1]{1,2,0:T(1,128)}), s32[16,32,1]{1,2,0:T(1,128)S(1)}, u32[]{:S(2)}, u32[]{:S(2)}) %all-to-all-start) | async-done | bytes 2080 | tf_op jit(solution)/shard_map/all_to_all | solution.py:75
  112.6 3.7 %all-to-all-start.3 = ((bf16[16,128,512]{2,1,0:T(8,128)(2,1)}), bf16[16,128,512]{2,1,0:T(8,128)(2,1)S(1)}, u32[]{:S(2)}, u32[]{:S(2)}) async-start(bf16[16,128,512]{2,1,0:T(8,128)(2,1)} %broadcast_in_dim.51), calls=%async_computation.3 | async-start | bytes 4194304 | tf_op jit(solution)/shard_map/all_to_all | solution.py:48
  116.4 3.8 %broadcast_select_fusion.1 = (bf16[512,1536]{1,0:T(8,128)(2,1)}, bf16[512,1536]{1,0:T(8,128)(2,1)}) fusion(bf16[512,1536]{1,0:T(8,128)(2,1)} %collective-permute-done.1, pred[]{:T(512)S(6)} %eq.21, bf16[1024,1536]{1,0:T(8,128)(2,1)} %copy-done.5), kind=kLoop, calls=%fused_computation.30 | loop fusion | flops 1572864 | bytes 6291457 | tf_op jit(solution)/shard_map/jit(_where)/select_n | solution.py:69
  125.3 3.9 %pad_maximum_fusion = bf16[512,16,2,96]{0,3,1,2:T(8,128)(2,1)} fusion(bf16[512,16,1,96]{0,3,1,2:T(8,128)(2,1)} %bitcast.48, bf16[512,16,1,96]{0,3,1,2:T(8,128)(2,1)} %bitcast.47), kind=kLoop, calls=%fused_computation.28 | loop fusion | flops 1572864 | bytes 6291456 | tf_op jit(solution)/shard_map/concatenate | solution.py:71
  129.2 11.2 %copy.19 = bf16[512,16,2,96]{3,2,1,0:T(2,128)(2,1)} copy(bf16[512,16,2,96]{0,3,1,2:T(8,128)(2,1)} %pad_maximum_fusion) | data formatting | bytes 6291456 | tf_op jit(solution)/shard_map/concatenate | solution.py:71
  140.4 12.4 %all_to_all.22 = bf16[16,32,3072]{2,1,0:T(8,128)(2,1)} reshape(bf16[512,16,2,96]{3,2,1,0:T(2,128)(2,1)} %copy.19) | data formatting | bytes 6291456 | tf_op jit(solution)/shard_map/all_to_all | solution.py:74
  152.8 7.2 %all-to-all-start.1 = ((bf16[16,32,3072]{2,1,0:T(8,128)(2,1)}), bf16[16,32,3072]{2,1,0:T(8,128)(2,1)}, u32[]{:S(2)}, u32[]{:S(2)}) async-start(bf16[16,32,3072]{2,1,0:T(8,128)(2,1)} %all_to_all.22), calls=%async_computation.1 | async-start | bytes 6291456 | tf_op jit(solution)/shard_map/all_to_all | solution.py:74
  162.4 42.2 %all-to-all-done.1 = bf16[16,32,3072]{2,1,0:T(8,128)(2,1)} async-done(((bf16[16,32,3072]{2,1,0:T(8,128)(2,1)}), bf16[16,32,3072]{2,1,0:T(8,128)(2,1)}, u32[]{:S(2)}, u32[]{:S(2)}) %all-to-all-start.1) | async-done | bytes 3145760 | tf_op jit(solution)/shard_map/all_to_all | solution.py:74
  210.0 4.6 %copy.20 = bf16[512,2560]{0,1:T(8,128)(2,1)} copy(bf16[512,2560]{1,0:T(8,128)(2,1)} %slice.33) | data formatting | bytes 5242880 | tf_op jit(solution)/shard_map/slice | solution.py:86
  216.3 70.5 %while.11 = (s32[]{:T(128)}, bf16[10,512,256]{1,2,0:T(8,128)(2,1)}, bf16[10,512,256]{1,2,0:T(8,128)(2,1)}, bf16[2560,256]{1,0:T(8,128)(2,1)}, bf16[2560,256]{1,0...) while((s32[]{:T(128)}, bf16[10,512,256]{1,2,0:T(8,128)(2,1)}, ...), condition=%wide.region_4.5_spmd.clone, body=%wide.region_1.4_spmd.clone.sunk | while | flops 1357904896 | bytes 24395376 | solution.py:42
  216.3 3.7 %fusion.38 = (f32[512]{0:T(512)S(1)}, f32[512,2560]{1,0:T(8,128)S(1)}) fusion(bf16[2560,256]{1,0:T(8,128)(2,1)} %get-tuple-element.160, bf16[10,512,256]{1,2,0:T(8,128)(2,1)} %get-tuple-element.159, s32[]{:T(128)} %get-tuple-element.149, pred[2560]{0:T(1024)(128)(4,1)S(1)} %get-tuple-element.163, s32[512]{0:T(512)S(1)} %get-tuple-element.162), kind=kOutput, calls=%fused_computation.43.clone.1 | convolution fusion | flops 680263168 | bytes 6822912 | tf_op jit(solution)/shard_map/while/body/eval_jaxpr/dot_general | solution.py:35
  230.4 3.7 %fusion.38 = (f32[512]{0:T(512)S(1)}, f32[512,2560]{1,0:T(8,128)S(1)}) fusion(bf16[2560,256]{1,0:T(8,128)(2,1)} %get-tuple-element.160, bf16[10,512,256]{1,2,0:T(8,128)(2,1)} %get-tuple-element.159, s32[]{:T(128)} %get-tuple-element.149, pred[2560]{0:T(1024)(128)(4,1)S(1)} %get-tuple-element.163, s32[512]{0:T(512)S(1)} %get-tuple-element.162), kind=kOutput, calls=%fused_computation.43.clone.1 | convolution fusion | flops 680263168 | bytes 6822912 | tf_op jit(solution)/shard_map/while/body/eval_jaxpr/dot_general | solution.py:35
  237.4 3.7 %fusion.38 = (f32[512]{0:T(512)S(1)}, f32[512,2560]{1,0:T(8,128)S(1)}) fusion(bf16[2560,256]{1,0:T(8,128)(2,1)} %get-tuple-element.160, bf16[10,512,256]{1,2,0:T(8,128)(2,1)} %get-tuple-element.159, s32[]{:T(128)} %get-tuple-element.149, pred[2560]{0:T(1024)(128)(4,1)S(1)} %get-tuple-element.163, s32[512]{0:T(512)S(1)} %get-tuple-element.162), kind=kOutput, calls=%fused_computation.43.clone.1 | convolution fusion | flops 680263168 | bytes 6822912 | tf_op jit(solution)/shard_map/while/body/eval_jaxpr/dot_general | solution.py:35
  244.5 3.7 %fusion.38 = (f32[512]{0:T(512)S(1)}, f32[512,2560]{1,0:T(8,128)S(1)}) fusion(bf16[2560,256]{1,0:T(8,128)(2,1)} %get-tuple-element.160, bf16[10,512,256]{1,2,0:T(8,128)(2,1)} %get-tuple-element.159, s32[]{:T(128)} %get-tuple-element.149, pred[2560]{0:T(1024)(128)(4,1)S(1)} %get-tuple-element.163, s32[512]{0:T(512)S(1)} %get-tuple-element.162), kind=kOutput, calls=%fused_computation.43.clone.1 | convolution fusion | flops 680263168 | bytes 6822912 | tf_op jit(solution)/shard_map/while/body/eval_jaxpr/dot_general | solution.py:35
  251.5 3.7 %fusion.38 = (f32[512]{0:T(512)S(1)}, f32[512,2560]{1,0:T(8,128)S(1)}) fusion(bf16[2560,256]{1,0:T(8,128)(2,1)} %get-tuple-element.160, bf16[10,512,256]{1,2,0:T(8,128)(2,1)} %get-tuple-element.159, s32[]{:T(128)} %get-tuple-element.149, pred[2560]{0:T(1024)(128)(4,1)S(1)} %get-tuple-element.163, s32[512]{0:T(512)S(1)} %get-tuple-element.162), kind=kOutput, calls=%fused_computation.43.clone.1 | convolution fusion | flops 680263168 | bytes 6822912 | tf_op jit(solution)/shard_map/while/body/eval_jaxpr/dot_general | solution.py:35
  265.6 3.7 %fusion.38 = (f32[512]{0:T(512)S(1)}, f32[512,2560]{1,0:T(8,128)S(1)}) fusion(bf16[2560,256]{1,0:T(8,128)(2,1)} %get-tuple-element.160, bf16[10,512,256]{1,2,0:T(8,128)(2,1)} %get-tuple-element.159, s32[]{:T(128)} %get-tuple-element.149, pred[2560]{0:T(1024)(128)(4,1)S(1)} %get-tuple-element.163, s32[512]{0:T(512)S(1)} %get-tuple-element.162), kind=kOutput, calls=%fused_computation.43.clone.1 | convolution fusion | flops 680263168 | bytes 6822912 | tf_op jit(solution)/shard_map/while/body/eval_jaxpr/dot_general | solution.py:35
  272.6 3.7 %fusion.38 = (f32[512]{0:T(512)S(1)}, f32[512,2560]{1,0:T(8,128)S(1)}) fusion(bf16[2560,256]{1,0:T(8,128)(2,1)} %get-tuple-element.160, bf16[10,512,256]{1,2,0:T(8,128)(2,1)} %get-tuple-element.159, s32[]{:T(128)} %get-tuple-element.149, pred[2560]{0:T(1024)(128)(4,1)S(1)} %get-tuple-element.163, s32[512]{0:T(512)S(1)} %get-tuple-element.162), kind=kOutput, calls=%fused_computation.43.clone.1 | convolution fusion | flops 680263168 | bytes 6822912 | tf_op jit(solution)/shard_map/while/body/eval_jaxpr/dot_general | solution.py:35
  279.7 3.7 %fusion.38 = (f32[512]{0:T(512)S(1)}, f32[512,2560]{1,0:T(8,128)S(1)}) fusion(bf16[2560,256]{1,0:T(8,128)(2,1)} %get-tuple-element.160, bf16[10,512,256]{1,2,0:T(8,128)(2,1)} %get-tuple-element.159, s32[]{:T(128)} %get-tuple-element.149, pred[2560]{0:T(1024)(128)(4,1)S(1)} %get-tuple-element.163, s32[512]{0:T(512)S(1)} %get-tuple-element.162), kind=kOutput, calls=%fused_computation.43.clone.1 | convolution fusion | flops 680263168 | bytes 6822912 | tf_op jit(solution)/shard_map/while/body/eval_jaxpr/dot_general | solution.py:35
  286.7 3.8 %fusion.18 = bf16[512,2560]{0,1:T(8,128)(2,1)} fusion(bf16[10,512,256]{1,2,0:T(8,128)(2,1)} %get-tuple-element.37, pred[512]{0:T(512)(128)(4,1)S(1)} %iota_compare_fusion.5), kind=kLoop, calls=%fused_computation.25 | loop fusion | flops 1310720 | bytes 5243392 | tf_op jit(solution)/shard_map/convert_element_type | solution.py:43
  290.5 4.4 %copy.23 = bf16[512,2560]{1,0:T(8,128)(2,1)} copy(bf16[512,2560]{0,1:T(8,128)(2,1)} %fusion.18) | data formatting | bytes 5242880 | tf_op jit(solution)/shard_map/convert_element_type | solution.py:43
  (92 shorter events, 68.9 us)
Async XLA Ops:
  6.5 4.5 %copy-start.8 = (f32[2560]{0:T(1024)S(1)}, f32[2560]{0:T(1024)}, u32[]{:S(2)}) copy-start(f32[2560]{0:T(1024)} %param.10) | copy-start | bytes 30724
  6.5 74.1 %all-gather.2.cloned.1.call-start = ((), (), s32[]{:S(2)}) async-start(), calls=%async_computation.4 | async-start | bytes 8355840 | tf_op jit(solution)/shard_map/all_gather | solution.py:63
  8.6 2.5 copy-start.2
  11.1 2.2 copy-start.7
  13.3 5.8 %collective-permute-start = (bf16[512,2560]{1,0:T(8,128)(2,1)}, bf16[512,2560]{1,0:T(8,128)(2,1)}, u32[]{:S(2)}, u32[]{:S(2)}) collective-permute-start(bf16[512,2560]{1,0:T(8,128)(2,1)} %fusion.13), channel_id=1, source_target_pairs={{0,16},{16,0},{32,48},{48,32},{64,80},{80,64},{96,112},{112,96},{1... | collective-permute-start | bytes 7864328 | tf_op jit(solution)/shard_map/ppermute | solution.py:59
  14.3 84.0 %all-to-all-start.2 = ((bf16[8,128,512]{2,1,0:T(8,128)(2,1)}), bf16[8,128,512]{2,1,0:T(8,128)(2,1)S(1)}, u32[]{:S(2)}, u32[]{:S(2)}) async-start(bf16[8,128,512]{2,1,0:T(8,128)(2,1)} %broadcast_in_dim.49), calls=%async_computation.2 | async-start | bytes 2097152 | tf_op jit(solution)/shard_map/all_to_all | solution.py:48
  92.9 1.6 copy-start.5
  94.5 1.8 copy-start.9
  95.8 20.6 %collective-permute-start.1 = (bf16[512,1536]{1,0:T(8,128)(2,1)}, bf16[512,1536]{1,0:T(8,128)(2,1)}, u32[]{:S(2)}, u32[]{:S(2)}) collective-permute-start(bf16[512,1536]{1,0:T(8,128)(2,1)} %slice.32), channel_id=1, source_target_pairs={{0,16},{16,0},{32,48},{48,32},{64,80},{80,64},{96,112},{112,96},{1... | collective-permute-start | bytes 4718600 | tf_op jit(solution)/shard_map/ppermute | solution.py:67
  98.3 12.8 %all-to-all-start = ((s32[16,32,1]{1,2,0:T(1,128)}), s32[16,32,1]{1,2,0:T(1,128)S(1)}, u32[]{:S(2)}, u32[]{:S(2)}) async-start(s32[16,32,1]{1,2,0:T(1,128)} %all_to_all.20), calls=%async_computation | async-start | bytes 16384 | tf_op jit(solution)/shard_map/all_to_all | solution.py:75
  112.6 40.2 %all-to-all-start.3 = ((bf16[16,128,512]{2,1,0:T(8,128)(2,1)}), bf16[16,128,512]{2,1,0:T(8,128)(2,1)S(1)}, u32[]{:S(2)}, u32[]{:S(2)}) async-start(bf16[16,128,512]{2,1,0:T(8,128)(2,1)} %broadcast_in_dim.51), calls=%async_computation.3 | async-start | bytes 4194304 | tf_op jit(solution)/shard_map/all_to_all | solution.py:48
  152.8 51.8 %all-to-all-start.1 = ((bf16[16,32,3072]{2,1,0:T(8,128)(2,1)}), bf16[16,32,3072]{2,1,0:T(8,128)(2,1)}, u32[]{:S(2)}, u32[]{:S(2)}) async-start(bf16[16,32,3072]{2,1,0:T(8,128)(2,1)} %all_to_all.22), calls=%async_computation.1 | async-start | bytes 6291456 | tf_op jit(solution)/shard_map/all_to_all | solution.py:74
  210.0 4.6 %copy-start.3 = (bf16[2048,256]{1,0:T(8,128)(2,1)S(1)}, bf16[2048,256]{1,0:T(8,128)(2,1)}, u32[]{:S(2)}) copy-start(bf16[2048,256]{1,0:T(8,128)(2,1)} %get-tuple-element.90) | copy-start | bytes 3145732
  210.0 4.6 %copy-start.4 = (bf16[2048,256]{1,0:T(8,128)(2,1)S(1)}, bf16[2048,256]{1,0:T(8,128)(2,1)}, u32[]{:S(2)}) copy-start(bf16[2048,256]{1,0:T(8,128)(2,1)} %get-tuple-element.91) | copy-start | bytes 3145732
  220.0 1.3 copy-start.6
  227.0 1.3 copy-start.6
  241.1 1.3 copy-start.6
  248.2 1.3 copy-start.6
  255.2 1.3 copy-start.6
  262.2 1.3 copy-start.6
  269.3 1.3 copy-start.6
  276.3 1.3 copy-start.6
  283.4 1.3 copy-start.6
  286.7 8.2 %copy-start.1 = (bf16[2560,192]{0,1:T(8,128)(2,1)S(1)}, bf16[2560,192]{0,1:T(8,128)(2,1)}, u32[]{:S(2)}) copy-start(bf16[2560,192]{0,1:T(8,128)(2,1)} %param.11) | copy-start | bytes 2949124
  (2 other events, 2.5 us)
Sparse Core Ops, SparseCore 0:
  9.5 71.1 all-gather.1
where the time goes:
time: 303 us; the launch traced here: 302 us
  waiting for transfers between devices  111 us (37%)
  matrix products  73.1 us (24%)
  local copies, waits for them, and re-layouts  54.7 us (18%)
  other arithmetic  26.8 us (9%)
  starting transfers between devices  20.9 us (7%)
  between operations  14.9 us (5%)
    all_gather x1, waiting for transfers between devices, shards(): w_gathered = lax.all_gather(w_mine, 'shard', axis=1, tiled=True)  61.6 us
    all_to_all x1, waiting for transfers between devices, shards(): lax.all_to_all(projected, 'shard', split_axis=0, concat_axis=0, tiled=True)  42.2 us
    dot_general x10, matrix products, one_head(): jnp.dot(head_q, keys.T, preferred_element_type=jnp.float32) * HD ** (-0.5)  37 us
    dot_general x10, matrix products, one_head(): return jnp.dot(weights, values, preferred_element_type=jnp.float32)  20.2 us
    all_to_all x1, local copies, waits for them, and re-layouts, shards(): lax.all_to_all(projected, 'shard', split_axis=0, concat_axis=0, tiled=True)  12.4 us
    dot_general x1, matrix products, shards(): jnp.dot(both, w_gathered, preferred_element_type=jnp.float32)  12.2 us
    concatenate x1, local copies, waits for them, and re-layouts, shards(): jnp.concatenate([half0, half1], axis=2).reshape(tok_dev, n_shard * cols)  11.2 us
    all_to_all x2, starting transfers between devices, gather_by_a2a(): return lax.all_to_all(spread, axis_name, 0, 0, tiled=True)  8.41 us
  transfers between devices with their start and end apart: 7, of which 3 were waited for; matrix products, arithmetic and copies ran while one was open for 16% of the time, Pallas kernels for 0%

commit v1 on v0

--- a/solution.py
+++ b/solution.py
@@ -2,6 +2,7 @@
 import jax.numpy as jnp
 from jax import lax
 from jax.sharding import PartitionSpec as P
+from jax.lax import axis_index, axis_size, ppermute
 
 H = 10
 HD = 256
@@ -60,7 +61,26 @@
     cols = w_qkv.shape[1]
     half = cols // 2
     w_mine = lax.dynamic_slice_in_dim(w_qkv, core * half, half, axis=1)
-    w_gathered = lax.all_gather(w_mine, "shard", axis=1, tiled=True)
+    formed, low, item_now = (axis_size("shard"), axis_index("shard"), w_mine.shape[1])
+    w_gathered = lax.dynamic_update_slice_in_dim(
+        jnp.zeros(
+            [q * formed if kk == 1 else q for kk, q in enumerate(w_mine.shape)], w_mine.dtype
+        ),
+        w_mine,
+        low * item_now,
+        axis=1,
+    )
+    x_now = moved = w_mine
+    for rr in range(1, formed // 2 + 1):
+        x_now = ppermute(x_now, "shard", [(kk, (kk + 1) % formed) for kk in range(formed)])
+        w_gathered = lax.dynamic_update_slice_in_dim(
+            w_gathered, x_now, (low - rr) % formed * item_now, axis=1
+        )
+        if 2 * rr < formed:
+            moved = ppermute(moved, "shard", [(kk, (kk - 1) % formed) for kk in range(formed)])
+            w_gathered = lax.dynamic_update_slice_in_dim(
+                w_gathered, moved, (low + rr) % formed * item_now, axis=1
+            )
     both = jnp.concatenate([normed, partner_rows], axis=0)
     out = jnp.dot(both, w_gathered, preferred_element_type=jnp.float32).astype(jnp.bfloat16)
     out_mine = out[:tok_dev]

time: 303 us -> 310 us (1.023)
  starting transfers between devices: 20.9 us -> 54.9 us
  between operations: 14.9 us -> 1.52 us
  matrix products: 73.1 us -> 64.3 us
  other arithmetic: 26.8 us -> 21.7 us
  waiting for transfers between devices: 111 us -> 106 us
  local copies, waits for them, and re-layouts: 54.7 us -> 59.5 us
    all_gather x1 -> x0, waiting for transfers between devices: 61.6 us -> none  [shards(): w_gathered = lax.all_gather(w_mine, 'shard', axis=1, tiled=True)]
    ppermute x0 -> x15, waiting for transfers between devices: none -> 53.2 us  [the longest x8 53.2 us: shards(): ppermute(x_now, 'shard', [(kk, (kk + 1) % formed) for kk in range(formed)])]
    ppermute x0 -> x15, starting transfers between devices: none -> 38.4 us  [the longest x7 36.8 us: shards(): ppermute(moved, 'shard', [(kk, (kk - 1) % formed) for kk in range(formed)])]
    dynamic_update_slice x0 -> x16, local copies, waits for them, and re-layouts: none -> 14.3 us  [the longest x8 7.58 us: shards(): lax.dynamic_update_slice_in_dim(w_gathered, x_now, (low - rr) % formed *...]
    dot_general x10, matrix products: 20.2 us -> 13.2 us  [one_head(): return jnp.dot(weights, values, preferred_element_type=jnp.float32)]
    all_to_all x2, waiting for transfers between devices: 0.01 us -> 3.51 us  [gather_by_a2a(): return lax.all_to_all(spread, axis_name, 0, 0, tiled=True)]
    all_to_all x1, starting transfers between devices: 7.2 us -> 3.74 us  [shards(): lax.all_to_all(projected, 'shard', split_axis=0, concat_axis=0, tiled=True)]
    slice x2, local copies, waits for them, and re-layouts: 6.25 us -> 2.82 us  [shards(): results = attend_request(placed[:, :HQ], placed[:, HQ:], prefix, lengths[0])]
  transfers between devices with their start and end apart: 7 -> 21, of which waited for: 3 -> 11; matrix products, arithmetic and copies ran while one was open for 16% -> 16% of each run, Pallas kernels for 0% -> 0%
where the time goes in v1:
time: 310 us; the launch traced here: 309 us
  waiting for transfers between devices  106 us (34%)
  matrix products  64.3 us (21%)
  local copies, waits for them, and re-layouts  59.5 us (19%)
  starting transfers between devices  54.9 us (18%)
  other arithmetic  21.7 us (7%)
    ppermute x8, waiting for transfers between devices, shards(): ppermute(x_now, 'shard', [(kk, (kk + 1) % formed) for kk in range(formed)])  53.2 us
    all_to_all x1, waiting for transfers between devices, shards(): lax.all_to_all(projected, 'shard', split_axis=0, concat_axis=0, tiled=True)  42.2 us
    dot_general x10, matrix products, one_head(): jnp.dot(head_q, keys.T, preferred_element_type=jnp.float32) * HD ** (-0.5)  37 us
    ppermute x7, starting transfers between devices, shards(): ppermute(moved, 'shard', [(kk, (kk - 1) % formed) for kk in range(formed)])  36.8 us
    dot_general x10, matrix products, one_head(): return jnp.dot(weights, values, preferred_element_type=jnp.float32)  13.2 us
    all_to_all x1, local copies, waits for them, and re-layouts, shards(): lax.all_to_all(projected, 'shard', split_axis=0, concat_axis=0, tiled=True)  12.4 us
    dot_general x1, matrix products, shards(): jnp.dot(both, w_gathered, preferred_element_type=jnp.float32)  12.2 us
    all_to_all x2, starting transfers between devices, gather_by_a2a(): return lax.all_to_all(spread, axis_name, 0, 0, tiled=True)  9.2 us
  transfers between devices with their start and end apart: 21, of which 11 were waited for; matrix products, arithmetic and copies ran while one was open for 16% of the time, Pallas kernels for 0%

profile of v1, /device:TPU:0, one launch (start us, length us, event | category | flops | bytes accessed | tf_op | source)
XLA Modules:
  0.0 308.6 jit_solution(12268934104127682869)
XLA Ops:
  3.8 4.7 %collective-permute-start.2 = (bf16[2560,96]{0,1:T(8,128)(2,1)}, bf16[2560,96]{0,1:T(8,128)(2,1)S(1)}, u32[]{:S(2)}, u32[]{:S(2)}) collective-permute-start(bf16[2560,96]{0,1:T(8,128)(2,1)} %get-tuple-element.85), channel_id=1, source_target_pairs={{0,15},{1,0},{2,1},{3,2},{4,3},{5,4},{6,5},{7,6},{8,7},{9,8},{10,9... | collective-permute-start | bytes 1474568 | tf_op jit(solution)/shard_map/ppermute | solution.py:80
  12.4 4.6 %all-to-all-start.2 = ((bf16[8,128,512]{2,1,0:T(8,128)(2,1)}), bf16[8,128,512]{2,1,0:T(8,128)(2,1)S(1)}, u32[]{:S(2)}, u32[]{:S(2)}) async-start(bf16[8,128,512]{2,1,0:T(8,128)(2,1)} %broadcast_in_dim.53), calls=%async_computation.2 | async-start | bytes 2097152 | tf_op jit(solution)/shard_map/all_to_all | solution.py:49
  20.1 5.3 %collective-permute-start.4 = (bf16[2560,96]{0,1:T(8,128)(2,1)S(1)}, bf16[2560,96]{0,1:T(8,128)(2,1)S(1)}, u32[]{:S(2)}, u32[]{:S(2)}) collective-permute-start(bf16[2560,96]{0,1:T(8,128)(2,1)S(1)} %collective-permute-done.2), channel_id=1, source_target_pairs={{0,15},{1,0},{2,1},{3,2},{4,3},{5,4},{6,5},{7,6},{8,7},{9,8},{10,9... | collective-permute-start | bytes 1474568 | tf_op jit(solution)/shard_map/ppermute | solution.py:80
  28.1 7.9 %collective-permute-done.3 = bf16[2560,96]{0,1:T(8,128)(2,1)S(1)} collective-permute-done((bf16[2560,96]{0,1:T(8,128)(2,1)}, bf16[2560,96]{0,1:T(8,128)(2,1)S(1)}, u32[]{:S(2)}, u32[]{:S(2)}) %collective-permute-start.3) | collective-permute-done | bytes 491552 | tf_op jit(solution)/shard_map/ppermute | solution.py:75
  36.0 5.3 %collective-permute-start.6 = (bf16[2560,96]{0,1:T(8,128)(2,1)S(1)}, bf16[2560,96]{0,1:T(8,128)(2,1)S(1)}, u32[]{:S(2)}, u32[]{:S(2)}) collective-permute-start(bf16[2560,96]{0,1:T(8,128)(2,1)S(1)} %collective-permute-done.4), channel_id=1, source_target_pairs={{0,15},{1,0},{2,1},{3,2},{4,3},{5,4},{6,5},{7,6},{8,7},{9,8},{10,9... | collective-permute-start | bytes 1474568 | tf_op jit(solution)/shard_map/ppermute | solution.py:80
  43.0 7.9 %collective-permute-done.5 = bf16[2560,96]{0,1:T(8,128)(2,1)S(1)} collective-permute-done((bf16[2560,96]{0,1:T(8,128)(2,1)S(1)}, bf16[2560,96]{0,1:T(8,128)(2,1)S(1)}, u32[]{:S(2)}, u32[]{:S(2)}) %collective-permute-start.5) | collective-permute-done | bytes 491552 | tf_op jit(solution)/shard_map/ppermute | solution.py:75
  50.9 5.3 %collective-permute-start.8 = (bf16[2560,96]{0,1:T(8,128)(2,1)S(1)}, bf16[2560,96]{0,1:T(8,128)(2,1)S(1)}, u32[]{:S(2)}, u32[]{:S(2)}) collective-permute-start(bf16[2560,96]{0,1:T(8,128)(2,1)S(1)} %collective-permute-done.6), channel_id=1, source_target_pairs={{0,15},{1,0},{2,1},{3,2},{4,3},{5,4},{6,5},{7,6},{8,7},{9,8},{10,9... | collective-permute-start | bytes 1474568 | tf_op jit(solution)/shard_map/ppermute | solution.py:80
  57.9 7.0 %collective-permute-done.7 = bf16[2560,96]{0,1:T(8,128)(2,1)S(1)} collective-permute-done((bf16[2560,96]{0,1:T(8,128)(2,1)S(1)}, bf16[2560,96]{0,1:T(8,128)(2,1)S(1)}, u32[]{:S(2)}, u32[]{:S(2)}) %collective-permute-start.7) | collective-permute-done | bytes 491552 | tf_op jit(solution)/shard_map/ppermute | solution.py:75
  64.9 5.3 %collective-permute-start.10 = (bf16[2560,96]{0,1:T(8,128)(2,1)S(1)}, bf16[2560,96]{0,1:T(8,128)(2,1)S(1)}, u32[]{:S(2)}, u32[]{:S(2)}) collective-permute-start(bf16[2560,96]{0,1:T(8,128)(2,1)S(1)} %collective-permute-done.8), channel_id=1, source_target_pairs={{0,15},{1,0},{2,1},{3,2},{4,3},{5,4},{6,5},{7,6},{8,7},{9,8},{10,9... | collective-permute-start | bytes 1474568 | tf_op jit(solution)/shard_map/ppermute | solution.py:80
  71.9 6.1 %collective-permute-done.9 = bf16[2560,96]{0,1:T(8,128)(2,1)S(1)} collective-permute-done((bf16[2560,96]{0,1:T(8,128)(2,1)S(1)}, bf16[2560,96]{0,1:T(8,128)(2,1)S(1)}, u32[]{:S(2)}, u32[]{:S(2)}) %collective-permute-start.9) | collective-permute-done | bytes 491552 | tf_op jit(solution)/shard_map/ppermute | solution.py:75
  78.0 5.3 %collective-permute-start.12 = (bf16[2560,96]{0,1:T(8,128)(2,1)S(1)}, bf16[2560,96]{0,1:T(8,128)(2,1)S(1)}, u32[]{:S(2)}, u32[]{:S(2)}) collective-permute-start(bf16[2560,96]{0,1:T(8,128)(2,1)S(1)} %collective-permute-done.10), channel_id=1, source_target_pairs={{0,15},{1,0},{2,1},{3,2},{4,3},{5,4},{6,5},{7,6},{8,7},{9,8},{10,9... | collective-permute-start | bytes 1474568 | tf_op jit(solution)/shard_map/ppermute | solution.py:80
  85.0 5.3 %collective-permute-done.11 = bf16[2560,96]{0,1:T(8,128)(2,1)S(1)} collective-permute-done((bf16[2560,96]{0,1:T(8,128)(2,1)S(1)}, bf16[2560,96]{0,1:T(8,128)(2,1)S(1)}, u32[]{:S(2)}, u32[]{:S(2)}) %collective-permute-start.11) | collective-permute-done | bytes 491552 | tf_op jit(solution)/shard_map/ppermute | solution.py:75
  90.3 5.3 %collective-permute-start.14 = (bf16[2560,96]{0,1:T(8,128)(2,1)S(1)}, bf16[2560,96]{0,1:T(8,128)(2,1)S(1)}, u32[]{:S(2)}, u32[]{:S(2)}) collective-permute-start(bf16[2560,96]{0,1:T(8,128)(2,1)S(1)} %collective-permute-done.12), channel_id=1, source_target_pairs={{0,15},{1,0},{2,1},{3,2},{4,3},{5,4},{6,5},{7,6},{8,7},{9,8},{10,9... | collective-permute-start | bytes 1474568 | tf_op jit(solution)/shard_map/ppermute | solution.py:80
  97.3 5.4 %collective-permute-done.13 = bf16[2560,96]{0,1:T(8,128)(2,1)S(1)} collective-permute-done((bf16[2560,96]{0,1:T(8,128)(2,1)S(1)}, bf16[2560,96]{0,1:T(8,128)(2,1)S(1)}, u32[]{:S(2)}, u32[]{:S(2)}) %collective-permute-start.13) | collective-permute-done | bytes 491552 | tf_op jit(solution)/shard_map/ppermute | solution.py:75
  104.3 10.5 %collective-permute-done.15 = bf16[2560,96]{0,1:T(8,128)(2,1)S(1)} collective-permute-done((bf16[2560,96]{0,1:T(8,128)(2,1)S(1)}, bf16[2560,96]{0,1:T(8,128)(2,1)S(1)}, u32[]{:S(2)}, u32[]{:S(2)}) %collective-permute-start.15) | collective-permute-done | bytes 491552 | tf_op jit(solution)/shard_map/ppermute | solution.py:75
  115.7 12.2 %fusion.19 = bf16[1024,1536]{1,0:T(8,128)(2,1)S(1)} fusion(bf16[2560,1536]{0,1:T(8,128)(2,1)} %constant_dynamic-update-slice_fusion, bf16[512,2560]{1,0:T(8,128)(2,1)} %collective-permute-done, bf16[512,2560]{1,0:T(8,128)(2,1)} %fusion.13), kind=kOutput, calls=%fused_computation.27 | convolution fusion | flops 8065122304 | bytes 16252928 | tf_op jit(solution)/shard_map/dot_general | solution.py:85
  135.8 7.4 %all-to-all-done = s32[16,32,1]{1,2,0:T(1,128)S(1)} async-done(((s32[16,32,1]{1,2,0:T(1,128)}), s32[16,32,1]{1,2,0:T(1,128)S(1)}, u32[]{:S(2)}, u32[]{:S(2)}) %all-to-all-start) | async-done | bytes 2080 | tf_op jit(solution)/shard_map/all_to_all | solution.py:95
  144.8 4.6 %all-to-all-start.3 = ((bf16[16,128,512]{2,1,0:T(8,128)(2,1)}), bf16[16,128,512]{2,1,0:T(8,128)(2,1)}, u32[]{:S(2)}, u32[]{:S(2)}) async-start(bf16[16,128,512]{2,1,0:T(8,128)(2,1)} %broadcast_in_dim.55), calls=%async_computation.3 | async-start | bytes 4194304 | tf_op jit(solution)/shard_map/all_to_all | solution.py:49
  156.9 7.8 %copy.19 = bf16[512,16,2,96]{3,2,1,0:T(2,128)(2,1)} copy(bf16[512,16,2,96]{0,3,1,2:T(8,128)(2,1)S(1)} %pad_maximum_fusion) | data formatting | bytes 6291456 | tf_op jit(solution)/shard_map/concatenate | solution.py:91
  164.7 12.4 %all_to_all.22 = bf16[16,32,3072]{2,1,0:T(8,128)(2,1)} reshape(bf16[512,16,2,96]{3,2,1,0:T(2,128)(2,1)} %copy.19) | data formatting | bytes 6291456 | tf_op jit(solution)/shard_map/all_to_all | solution.py:94
  180.6 3.7 %all-to-all-start.1 = ((bf16[16,32,3072]{2,1,0:T(8,128)(2,1)}), bf16[16,32,3072]{2,1,0:T(8,128)(2,1)S(1)}, u32[]{:S(2)}, u32[]{:S(2)}) async-start(bf16[16,32,3072]{2,1,0:T(8,128)(2,1)} %all_to_all.22), calls=%async_computation.1 | async-start | bytes 6291456 | tf_op jit(solution)/shard_map/all_to_all | solution.py:94
  188.2 42.2 %all-to-all-done.1 = bf16[16,32,3072]{2,1,0:T(8,128)(2,1)S(1)} async-done(((bf16[16,32,3072]{2,1,0:T(8,128)(2,1)}), bf16[16,32,3072]{2,1,0:T(8,128)(2,1)S(1)}, u32[]{:S(2)}, u32[]{:S(2)}) %all-to-all-start.1) | async-done | bytes 3145760 | tf_op jit(solution)/shard_map/all_to_all | solution.py:94
  238.5 63.7 %while.11 = (s32[]{:T(128)}, bf16[10,512,256]{1,2,0:T(8,128)(2,1)S(1)}, bf16[10,512,256]{1,2,0:T(8,128)(2,1)}, bf16[2560,256]{1,0:T(8,128)(2,1)}, bf16[2560,256]...) while((s32[]{:T(128)}, bf16[10,512,256]{1,2,0:T(8,128)(2,1)S(1)}, ...), condition=%wide.region_4.5_spmd.clone, body=%wide.region_1.4_spmd.clone.sunk | while | flops 1357904896 | bytes 24394868 | solution.py:43
  244.8 3.7 %fusion.38 = (f32[512]{0:T(512)S(1)}, f32[512,2560]{1,0:T(8,128)S(1)}) fusion(bf16[2560,256]{1,0:T(8,128)(2,1)} %get-tuple-element.162, bf16[10,512,256]{1,2,0:T(8,128)(2,1)} %get-tuple-element.161, s32[]{:T(128)} %get-tuple-element.151, pred[2560]{0:T(1024)(128)(4,1)S(1)} %get-tuple-element.165, s32[512]{0:T(512)S(1)} %get-tuple-element.164), kind=kOutput, calls=%fused_computation.59.clone.1 | convolution fusion | flops 680263168 | bytes 6822912 | tf_op jit(solution)/shard_map/while/body/eval_jaxpr/dot_general | solution.py:36
  (135 shorter events, 121.2 us)
Async XLA Ops:
  0.0 9.2 %copy-start.8 = (f32[2560]{0:T(1024)S(1)}, f32[2560]{0:T(1024)}, u32[]{:S(2)}) copy-start(f32[2560]{0:T(1024)} %param.10) | copy-start | bytes 30724
  1.4 10.0 %copy-start.7 = (bf16[1,128,512]{2,1,0:T(8,128)(2,1)S(1)}, bf16[1,128,512]{2,1,0:T(8,128)(2,1)}, u32[]{:S(2)}) copy-start(bf16[1,128,512]{2,1,0:T(8,128)(2,1)} %param.12) | copy-start | bytes 393220
  2.2 17.9 %collective-permute-start.1 = (bf16[2560,96]{0,1:T(8,128)(2,1)}, bf16[2560,96]{0,1:T(8,128)(2,1)}, u32[]{:S(2)}, u32[]{:S(2)}) collective-permute-start(bf16[2560,96]{0,1:T(8,128)(2,1)} %get-tuple-element.85), channel_id=1, source_target_pairs={{0,1},{1,2},{2,3},{3,4},{4,5},{5,6},{6,7},{7,8},{8,9},{9,10},{10,1... | collective-permute-start | bytes 1474568 | tf_op jit(solution)/shard_map/ppermute | solution.py:75
  3.8 16.3 %collective-permute-start.2 = (bf16[2560,96]{0,1:T(8,128)(2,1)}, bf16[2560,96]{0,1:T(8,128)(2,1)S(1)}, u32[]{:S(2)}, u32[]{:S(2)}) collective-permute-start(bf16[2560,96]{0,1:T(8,128)(2,1)} %get-tuple-element.85), channel_id=1, source_target_pairs={{0,15},{1,0},{2,1},{3,2},{4,3},{5,4},{6,5},{7,6},{8,7},{9,8},{10,9... | collective-permute-start | bytes 1474568 | tf_op jit(solution)/shard_map/ppermute | solution.py:80
  11.3 104.3 %collective-permute-start = (bf16[512,2560]{1,0:T(8,128)(2,1)}, bf16[512,2560]{1,0:T(8,128)(2,1)}, u32[]{:S(2)}, u32[]{:S(2)}) collective-permute-start(bf16[512,2560]{1,0:T(8,128)(2,1)} %fusion.13), channel_id=1, source_target_pairs={{0,16},{16,0},{32,48},{48,32},{64,80},{80,64},{96,112},{112,96},{1... | collective-permute-start | bytes 7864328 | tf_op jit(solution)/shard_map/ppermute | solution.py:60
  12.4 119.9 %all-to-all-start.2 = ((bf16[8,128,512]{2,1,0:T(8,128)(2,1)}), bf16[8,128,512]{2,1,0:T(8,128)(2,1)S(1)}, u32[]{:S(2)}, u32[]{:S(2)}) async-start(bf16[8,128,512]{2,1,0:T(8,128)(2,1)} %broadcast_in_dim.53), calls=%async_computation.2 | async-start | bytes 2097152 | tf_op jit(solution)/shard_map/all_to_all | solution.py:49
  20.1 15.9 %collective-permute-start.3 = (bf16[2560,96]{0,1:T(8,128)(2,1)}, bf16[2560,96]{0,1:T(8,128)(2,1)S(1)}, u32[]{:S(2)}, u32[]{:S(2)}) collective-permute-start(bf16[2560,96]{0,1:T(8,128)(2,1)} %collective-permute-done.1), channel_id=1, source_target_pairs={{0,1},{1,2},{2,3},{3,4},{4,5},{5,6},{6,7},{7,8},{8,9},{9,10},{10,1... | collective-permute-start | bytes 1474568 | tf_op jit(solution)/shard_map/ppermute | solution.py:75
  20.1 15.9 %collective-permute-start.4 = (bf16[2560,96]{0,1:T(8,128)(2,1)S(1)}, bf16[2560,96]{0,1:T(8,128)(2,1)S(1)}, u32[]{:S(2)}, u32[]{:S(2)}) collective-permute-start(bf16[2560,96]{0,1:T(8,128)(2,1)S(1)} %collective-permute-done.2), channel_id=1, source_target_pairs={{0,15},{1,0},{2,1},{3,2},{4,3},{5,4},{6,5},{7,6},{8,7},{9,8},{10,9... | collective-permute-start | bytes 1474568 | tf_op jit(solution)/shard_map/ppermute | solution.py:80
  36.0 14.8 %collective-permute-start.5 = (bf16[2560,96]{0,1:T(8,128)(2,1)S(1)}, bf16[2560,96]{0,1:T(8,128)(2,1)S(1)}, u32[]{:S(2)}, u32[]{:S(2)}) collective-permute-start(bf16[2560,96]{0,1:T(8,128)(2,1)S(1)} %collective-permute-done.3), channel_id=1, source_target_pairs={{0,1},{1,2},{2,3},{3,4},{4,5},{5,6},{6,7},{7,8},{8,9},{9,10},{10,1... | collective-permute-start | bytes 1474568 | tf_op jit(solution)/shard_map/ppermute | solution.py:75
  36.0 14.8 %collective-permute-start.6 = (bf16[2560,96]{0,1:T(8,128)(2,1)S(1)}, bf16[2560,96]{0,1:T(8,128)(2,1)S(1)}, u32[]{:S(2)}, u32[]{:S(2)}) collective-permute-start(bf16[2560,96]{0,1:T(8,128)(2,1)S(1)} %collective-permute-done.4), channel_id=1, source_target_pairs={{0,15},{1,0},{2,1},{3,2},{4,3},{5,4},{6,5},{7,6},{8,7},{9,8},{10,9... | collective-permute-start | bytes 1474568 | tf_op jit(solution)/shard_map/ppermute | solution.py:80
  50.9 14.0 %collective-permute-start.7 = (bf16[2560,96]{0,1:T(8,128)(2,1)S(1)}, bf16[2560,96]{0,1:T(8,128)(2,1)S(1)}, u32[]{:S(2)}, u32[]{:S(2)}) collective-permute-start(bf16[2560,96]{0,1:T(8,128)(2,1)S(1)} %collective-permute-done.5), channel_id=1, source_target_pairs={{0,1},{1,2},{2,3},{3,4},{4,5},{5,6},{6,7},{7,8},{8,9},{9,10},{10,1... | collective-permute-start | bytes 1474568 | tf_op jit(solution)/shard_map/ppermute | solution.py:75
  50.9 14.0 %collective-permute-start.8 = (bf16[2560,96]{0,1:T(8,128)(2,1)S(1)}, bf16[2560,96]{0,1:T(8,128)(2,1)S(1)}, u32[]{:S(2)}, u32[]{:S(2)}) collective-permute-start(bf16[2560,96]{0,1:T(8,128)(2,1)S(1)} %collective-permute-done.6), channel_id=1, source_target_pairs={{0,15},{1,0},{2,1},{3,2},{4,3},{5,4},{6,5},{7,6},{8,7},{9,8},{10,9... | collective-permute-start | bytes 1474568 | tf_op jit(solution)/shard_map/ppermute | solution.py:80
  64.9 13.1 %collective-permute-start.9 = (bf16[2560,96]{0,1:T(8,128)(2,1)S(1)}, bf16[2560,96]{0,1:T(8,128)(2,1)S(1)}, u32[]{:S(2)}, u32[]{:S(2)}) collective-permute-start(bf16[2560,96]{0,1:T(8,128)(2,1)S(1)} %collective-permute-done.7), channel_id=1, source_target_pairs={{0,1},{1,2},{2,3},{3,4},{4,5},{5,6},{6,7},{7,8},{8,9},{9,10},{10,1... | collective-permute-start | bytes 1474568 | tf_op jit(solution)/shard_map/ppermute | solution.py:75
  64.9 13.1 %collective-permute-start.10 = (bf16[2560,96]{0,1:T(8,128)(2,1)S(1)}, bf16[2560,96]{0,1:T(8,128)(2,1)S(1)}, u32[]{:S(2)}, u32[]{:S(2)}) collective-permute-start(bf16[2560,96]{0,1:T(8,128)(2,1)S(1)} %collective-permute-done.8), channel_id=1, source_target_pairs={{0,15},{1,0},{2,1},{3,2},{4,3},{5,4},{6,5},{7,6},{8,7},{9,8},{10,9... | collective-permute-start | bytes 1474568 | tf_op jit(solution)/shard_map/ppermute | solution.py:80
  78.0 12.3 %collective-permute-start.11 = (bf16[2560,96]{0,1:T(8,128)(2,1)S(1)}, bf16[2560,96]{0,1:T(8,128)(2,1)S(1)}, u32[]{:S(2)}, u32[]{:S(2)}) collective-permute-start(bf16[2560,96]{0,1:T(8,128)(2,1)S(1)} %collective-permute-done.9), channel_id=1, source_target_pairs={{0,1},{1,2},{2,3},{3,4},{4,5},{5,6},{6,7},{7,8},{8,9},{9,10},{10,1... | collective-permute-start | bytes 1474568 | tf_op jit(solution)/shard_map/ppermute | solution.py:75
  78.0 12.3 %collective-permute-start.12 = (bf16[2560,96]{0,1:T(8,128)(2,1)S(1)}, bf16[2560,96]{0,1:T(8,128)(2,1)S(1)}, u32[]{:S(2)}, u32[]{:S(2)}) collective-permute-start(bf16[2560,96]{0,1:T(8,128)(2,1)S(1)} %collective-permute-done.10), channel_id=1, source_target_pairs={{0,15},{1,0},{2,1},{3,2},{4,3},{5,4},{6,5},{7,6},{8,7},{9,8},{10,9... | collective-permute-start | bytes 1474568 | tf_op jit(solution)/shard_map/ppermute | solution.py:80
  90.3 12.4 %collective-permute-start.13 = (bf16[2560,96]{0,1:T(8,128)(2,1)S(1)}, bf16[2560,96]{0,1:T(8,128)(2,1)S(1)}, u32[]{:S(2)}, u32[]{:S(2)}) collective-permute-start(bf16[2560,96]{0,1:T(8,128)(2,1)S(1)} %collective-permute-done.11), channel_id=1, source_target_pairs={{0,1},{1,2},{2,3},{3,4},{4,5},{5,6},{6,7},{7,8},{8,9},{9,10},{10,1... | collective-permute-start | bytes 1474568 | tf_op jit(solution)/shard_map/ppermute | solution.py:75
  90.3 13.2 %collective-permute-start.14 = (bf16[2560,96]{0,1:T(8,128)(2,1)S(1)}, bf16[2560,96]{0,1:T(8,128)(2,1)S(1)}, u32[]{:S(2)}, u32[]{:S(2)}) collective-permute-start(bf16[2560,96]{0,1:T(8,128)(2,1)S(1)} %collective-permute-done.12), channel_id=1, source_target_pairs={{0,15},{1,0},{2,1},{3,2},{4,3},{5,4},{6,5},{7,6},{8,7},{9,8},{10,9... | collective-permute-start | bytes 1474568 | tf_op jit(solution)/shard_map/ppermute | solution.py:80
  102.7 12.2 %collective-permute-start.15 = (bf16[2560,96]{0,1:T(8,128)(2,1)S(1)}, bf16[2560,96]{0,1:T(8,128)(2,1)S(1)}, u32[]{:S(2)}, u32[]{:S(2)}) collective-permute-start(bf16[2560,96]{0,1:T(8,128)(2,1)S(1)} %collective-permute-done.13), channel_id=1, source_target_pairs={{0,1},{1,2},{2,3},{3,4},{4,5},{5,6},{6,7},{7,8},{8,9},{9,10},{10,1... | collective-permute-start | bytes 1474568 | tf_op jit(solution)/shard_map/ppermute | solution.py:75
  115.7 14.6 %copy-start.9 = (s32[1,512]{1,0:T(1,128)S(1)}, s32[1,512]{1,0:T(1,128)}, u32[]{:S(2)}) copy-start(s32[1,512]{1,0:T(1,128)} %param.15) | copy-start | bytes 6148
  129.7 19.7 %collective-permute-start.16 = (bf16[512,1536]{1,0:T(8,128)(2,1)S(1)}, bf16[512,1536]{1,0:T(8,128)(2,1)}, u32[]{:S(2)}, u32[]{:S(2)}) collective-permute-start(bf16[512,1536]{1,0:T(8,128)(2,1)S(1)} %slice.32), channel_id=1, source_target_pairs={{0,16},{16,0},{32,48},{48,32},{64,80},{80,64},{96,112},{112,96},{1... | collective-permute-start | bytes 4718600 | tf_op jit(solution)/shard_map/ppermute | solution.py:87
  132.3 10.9 %all-to-all-start = ((s32[16,32,1]{1,2,0:T(1,128)}), s32[16,32,1]{1,2,0:T(1,128)S(1)}, u32[]{:S(2)}, u32[]{:S(2)}) async-start(s32[16,32,1]{1,2,0:T(1,128)} %all_to_all.20), calls=%async_computation | async-start | bytes 16384 | tf_op jit(solution)/shard_map/all_to_all | solution.py:95
  144.8 35.9 %all-to-all-start.3 = ((bf16[16,128,512]{2,1,0:T(8,128)(2,1)}), bf16[16,128,512]{2,1,0:T(8,128)(2,1)}, u32[]{:S(2)}, u32[]{:S(2)}) async-start(bf16[16,128,512]{2,1,0:T(8,128)(2,1)} %broadcast_in_dim.55), calls=%async_computation.3 | async-start | bytes 4194304 | tf_op jit(solution)/shard_map/all_to_all | solution.py:49
  180.6 49.7 %all-to-all-start.1 = ((bf16[16,32,3072]{2,1,0:T(8,128)(2,1)}), bf16[16,32,3072]{2,1,0:T(8,128)(2,1)S(1)}, u32[]{:S(2)}, u32[]{:S(2)}) async-start(bf16[16,32,3072]{2,1,0:T(8,128)(2,1)} %all_to_all.22), calls=%async_computation.1 | async-start | bytes 6291456 | tf_op jit(solution)/shard_map/all_to_all | solution.py:94
  (16 other events, 38.8 us)
